TPU v7x, 32 devices: a whole 2x2x4 slice. The times are simulated.
32 devices in a mesh: row: 4 (over z), col: 8 (over y, x, core).
Axes of the slice: x: 2, y: 2, z: 4, core: 2. Of those that a mesh axis runs over, the one named last changes fastest.
Arguments:
- factor_rows: float32 [2, 1024, 4096], P(None, 'col', 'row'), as said below
- adjoint_rows: float32 [2, 1024, 4096], P(None, 'col', 'row'), as said below
- panel_inverse: float32 [2, 1024, 1024], replicated, as said below
Outputs:
- kernel_adjoint: float32 [2, 1024, 4096], P(None, 'col', 'row')
Inputs may be any that keep to these rules, and one draw needn't show every extreme that they name: `factor_rows`: zero right of the diagonal; in panel p the columns J_p hold a lower-triangular block with diagonal entries from 0.5 to 4. `adjoint_rows`: zero right of the diagonal of the same rows. panel_inverse[p] is the inverse of factor_rows[p, :, J_p] to float32 rounding.
All inputs are finite; a program needn't handle non-finite values.
Results may differ from a plain program's by a relative error of at most 0.0001.
Values sent between devices are 32-bit elements; how exact they have to be, the bound alone decides.
No kernel may reach another device: no remote copies, remote signals or barrier semaphores. Data moves between devices by JAX's collectives and lax.ppermute only.
A program may use at most 128 MiB of HBM per device.

v0:
```python
import jax
import jax.numpy as jnp
from jax import lax
from jax.sharding import PartitionSpec as P

HIGHEST = lax.Precision.HIGHEST


def spread(value, axis, source):
    kept = jnp.where(lax.axis_index(axis) == source, value, 0).astype(value.dtype)
    return lax.psum(kept, axis)


def phi_lower(matrix):
    unit_diag = jnp.eye(matrix.shape[0], dtype=jnp.float32)
    return jnp.tril(matrix) * (1.0 - 0.5 * unit_diag)


def product(left_mat, right_mat):
    return jnp.dot(left_mat, right_mat, precision=HIGHEST, preferred_element_type=jnp.float32)


def diag_fix(factor, diag_pre, inverse):
    inner = phi_lower(product(factor.T, diag_pre))
    return phi_lower(product(product(inverse.T, inner + inner.T), inverse))


def fixed_block(factor, diag_term, inverse):
    diag_pre = jnp.tril(lax.psum(diag_term, "col"))
    return diag_fix(factor, diag_pre, inverse)


def local(factor_rows, adjoint_rows, panel_inverse):
    row_count = lax.axis_size("row")
    panels = panel_inverse.shape[0]
    panel_width = panel_inverse.shape[1]
    slab_rows = factor_rows.shape[1]
    span_cols = factor_rows.shape[2]
    row_pos = lax.axis_index("row")
    col_pos = lax.axis_index("col")
    first_col = (row_count - panels) * panel_width
    columns = row_pos * span_cols + jnp.arange(span_cols, dtype=jnp.int32)
    offset = col_pos * slab_rows
    adjoint = adjoint_rows
    for panel in range(panels - 1, -1, -1):
        owner_row = row_count - panels + panel
        is_owner = row_pos == owner_row
        inverse = panel_inverse[panel]
        held_adj, held_fac = (
            spread(adjoint[panel:], "row", owner_row),
            spread(factor_rows[panel:], "row", owner_row),
        )
        col_adjoint = jnp.einsum("qib,bj->qij", held_adj[1:], inverse, precision=HIGHEST)
        placed = lax.dynamic_update_slice(
            jnp.zeros((panel_width, panel_width), jnp.float32), held_adj[0], (offset, 0)
        )
        diag_term = placed - jnp.einsum("qbi,qbj->ij", col_adjoint, held_fac[1:], precision=HIGHEST)
        row_panel = lax.all_gather(factor_rows[panel], "col", axis=0, tiled=True)
        diag_factor = lax.all_gather(held_fac[0], "col", axis=0, tiled=True)
        diag_new = fixed_block(diag_factor, diag_term, inverse)
        sym_rows = lax.dynamic_slice_in_dim(diag_new + diag_new.T, offset, slab_rows, 0)
        left_cols = (columns < first_col + panel * panel_width)[None, :]
        row_update = product(sym_rows, row_panel)
        pieces = [adjoint[:panel]]
        if panel + 1 < panels:
            later_rows = factor_rows[panel + 1 :]
            row_update = (
                lax.psum_scatter(
                    jnp.einsum("qbi,qbj->ij", col_adjoint, later_rows, precision=HIGHEST),
                    "col",
                    scatter_dimension=0,
                    tiled=True,
                )
                + row_update
            )
            block_update = jnp.einsum("qib,bj->qij", col_adjoint, row_panel, precision=HIGHEST)
            lower_new = jnp.where(
                left_cols[None], adjoint[panel + 1 :] - block_update, adjoint[panel + 1 :]
            )
            lower_new = jnp.where(is_owner, col_adjoint, lower_new)
        own_new = jnp.where(left_cols, adjoint[panel] - row_update, adjoint[panel])
        own_new = jnp.where(
            is_owner, lax.dynamic_slice_in_dim(diag_new, offset, slab_rows, 0), own_new
        )
        pieces.append(own_new[None])
        if panel + 1 < panels:
            pieces.append(lower_new)
        adjoint = jnp.concatenate(pieces, axis=0)
    return adjoint


def solution(mesh):
    return jax.shard_map(
        local,
        mesh=mesh,
        in_specs=(P(None, "col", "row"), P(None, "col", "row"), P()),
        out_specs=P(None, "col", "row"),
        check_vma=False,
    )
```

profile of v0, /device:TPU:0, one launch (start us, length us, event | category | flops | bytes accessed | tf_op | source)
XLA Modules:
  0.0 607.5 jit_solution(6495797042716820309)
XLA Ops:
  6.5 1.5 copy.4
  8.1 1.3 fusion.112
  9.4 0.2 copy.23
  9.6 1.0 select_bitcast_fusion.1
  10.6 0.8 select_bitcast_fusion
  11.5 0.0 all-reduce.7.cloned.1.call-start
  11.5 55.0 %all-reduce.13.cloned.1.call-done = (f32[128,1024]{0,1:T(8,128)}, f32[128,1024]{0,1:T(8,128)}) async-done(((f32[128,1024]{0,1:T(8,128)}, f32[128,1024]{0,1:T(8,128)}), (f32[128,1024]{0,1:T(8,128)}, f32[128,1024]{0,1:T(8,128)})) %all-reduce.13.cloned.1.call-update) | async-done | bytes 1048592 | tf_op jit(solution)/shard_map/psum | solution.py:11
  66.5 2.5 broadcast.53.clone
  69.0 0.9 constant_dynamic-update-slice_fusion
  69.9 0.7 all-gather.8.cloned.1.call-update
  70.7 0.5 all-gather.12.cloned.1.call-update
  71.3 0.2 copy.22
  71.5 1.3 iota_compare_fusion.1
  72.7 1.1 broadcast_select_fusion
  73.8 76.7 %all-reduce.7.cloned.1.call-done = f32[1024,1024]{0,1:T(8,128)} async-done(((f32[1024,1024]{0,1:T(8,128)}), f32[1024,1024]{0,1:T(8,128)}) %all-reduce.7.cloned.1.call-update) | async-done | bytes 4194320 | tf_op jit(solution)/shard_map/psum | solution.py:29
  150.6 39.4 %all-gather.8.cloned.1.call-done = f32[1024,1024]{0,1:T(8,128)} async-done(((f32[128,1024]{0,1:T(8,128)}), f32[1024,1024]{0,1:T(8,128)}) %all-gather.8.cloned.1.call-update) | async-done | bytes 4194320 | tf_op jit(solution)/shard_map/all_gather | solution.py:59
  190.0 17.9 %fusion.29 = f32[1024,1024]{1,0:T(8,128)} fusion(f32[1024,1024]{0,1:T(8,128)} %all-gather.8.cloned.1.call-done, f32[1024,1024]{0,1:T(8,128)} %all-reduce.7.cloned.1.call-done), kind=kOutput, calls=%fused_computation.36 | convolution fusion | flops 12886999040 | bytes 12582912 | tf_op jit(solution)/shard_map/dot_general | solution.py:20
  207.8 5.3 copy.8
  213.2 20.0 %fusion.17 = f32[1024,1024]{1,0:T(8,128)S(1)} fusion(f32[1024,1024]{1,0:T(8,128)} %fusion.29, f32[1024,1024]{0,1:T(8,128)} %copy.8, f32[2,1024,1024]{2,1,0:T(8,128)} %param.5), kind=kOutput, calls=%fused_computation.17 | convolution fusion | flops 12898533376 | bytes 16777216 | tf_op jit(solution)/shard_map/dot_general | solution.py:20
  233.2 17.1 %fusion.15 = f32[1024,1024]{1,0:T(8,128)} fusion(f32[1024,1024]{1,0:T(8,128)S(1)} %fusion.17, f32[2,1024,1024]{2,1,0:T(8,128)} %param.5), kind=kOutput, calls=%fused_computation.15 | convolution fusion | flops 12884901888 | bytes 12582912 | tf_op jit(solution)/shard_map/dot_general | solution.py:20
  250.3 5.3 copy.9
  255.7 6.5 %select_multiply_fusion.1 = (f32[1024,1024]{0,1:T(8,128)}, f32[1024,1024]{0,1:T(8,128)}) fusion(f32[1024,1024]{0,1:T(8,128)} %copy.9), kind=kLoop, calls=%fused_computation.28 | loop fusion | flops 9437184 | bytes 12582912 | tf_op jit(solution)/shard_map/mul | solution.py:16
  262.2 6.2 %fusion.50 = f32[128,1024]{0,1:T(8,128)S(1)} fusion(f32[1,1024,1024]{1,2,0:T(8,128)} %all-gather.12.cloned.1.call-done, f32[1024,1024]{0,1:T(8,128)} %bitcast.96, s32[]{:T(128)S(6)} %select_n.105, f32[1024,1024]{0,1:T(8,128)} %get-tuple-element.13, f32[1,128,1024]{1,2,0:T(8,128)S(1)} %copy.23, f32[1024,1024]{0,1:T(8,128)} %get-tuple-element.14, ...), kind=kOutput, calls=%fused_computation.55 | convolution fusion | flops 1611399168 | bytes 7473664 | tf_op jit(solution)/shard_map/dot_general | solution.py:20
  268.4 1.1 maximum_select_fusion
  269.5 1.9 slice.43
  271.4 0.2 all-reduce.9.cloned.1.call-start
  271.7 85.6 %all-reduce.11.cloned.1.call-done = (f32[2,128,1024]{1,2,0:T(8,128)}, f32[2,128,1024]{1,2,0:T(8,128)}) async-done(((f32[2,128,1024]{1,2,0:T(8,128)}, f32[2,128,1024]{1,2,0:T(8,128)}), (f32[2,128,1024]{1,2,0:T(8,128)}, f32[2,128,1024]{1,2,0:T(8,128)})) %all-reduce.11.cloned.1.call-update) | async-done | bytes 2097168 | tf_op jit(solution)/shard_map/psum | solution.py:11
  357.2 0.5 broadcast.53
  357.7 0.7 copy-done.1
  358.4 0.1 fusion.84
  358.5 4.8 fusion.11
  363.3 5.1 convolution_subtract_fusion
  368.5 1.9 slice.44
  370.4 5.0 fusion.89
  375.5 0.2 copy.16
  375.7 19.2 %all-gather.14.cloned.1.call-done = f32[1,1024,1024]{2,1,0:T(8,128)} async-done(((f32[1,128,1024]{2,1,0:T(8,128)}), f32[1,1024,1024]{2,1,0:T(8,128)}) %all-gather.14.cloned.1.call-update) | async-done | bytes 4194320 | tf_op jit(solution)/shard_map/all_gather | solution.py:58
  394.8 8.7 %fusion.65 = f32[1,128,1024]{1,2,0:T(8,128)S(1)} fusion(f32[128,1024]{0,1:T(8,128)S(1)} %copy.16, f32[128,1024]{0,1:T(8,128)S(1)} %fusion.50, f32[128,1024]{1,0:T(8,128)S(1)} %fusion.11, f32[1,1024,1024]{2,1,0:T(8,128)} %all-gather.14.cloned.1.call-done, pred[1024]{0:T(1024)(128)(4,1)S(1)} %fusion.97, pred[]{:T(512)S(6)} %eq.34), kind=kOutput, calls=%fused_computation.60 | convolution fusion | flops 1611005952 | bytes 6292481 | tf_op jit(solution)/shard_map/qib,bj->qij/dot_general | solution.py:76
  403.5 76.0 %all-reduce.9.cloned.1.call-done = f32[1024,1024]{0,1:T(8,128)} async-done(((f32[1024,1024]{0,1:T(8,128)}), f32[1024,1024]{0,1:T(8,128)}) %all-reduce.9.cloned.1.call-update) | async-done | bytes 4194320 | tf_op jit(solution)/shard_map/psum | solution.py:29
  479.5 39.4 %all-gather.10.cloned.1.call-done = f32[1,1024,1024]{1,2,0:T(8,128)} async-done(((f32[1,128,1024]{1,2,0:T(8,128)}), f32[1,1024,1024]{1,2,0:T(8,128)}) %all-gather.10.cloned.1.call-update) | async-done | bytes 4194320 | tf_op jit(solution)/shard_map/all_gather | solution.py:59
  518.9 17.9 %fusion.22 = f32[1024,1024]{1,0:T(8,128)} fusion(f32[1,1024,1024]{1,2,0:T(8,128)} %all-gather.10.cloned.1.call-done, f32[1024,1024]{0,1:T(8,128)} %all-reduce.9.cloned.1.call-done), kind=kOutput, calls=%fused_computation.22 | convolution fusion | flops 12886999040 | bytes 12582912 | tf_op jit(solution)/shard_map/dot_general | solution.py:20
  536.8 5.3 copy.11
  542.1 20.4 %fusion.6 = f32[1024,1024]{1,0:T(8,128)S(1)} fusion(f32[1024,1024]{1,0:T(8,128)} %fusion.22, f32[1024,1024]{0,1:T(8,128)} %copy.11, f32[2,1024,1024]{2,1,0:T(8,128)} %param.5), kind=kOutput, calls=%fused_computation.7 | convolution fusion | flops 12898533376 | bytes 16777216 | tf_op jit(solution)/shard_map/dot_general | solution.py:20
  562.5 17.0 %fusion.8 = f32[1024,1024]{1,0:T(8,128)} fusion(f32[1024,1024]{1,0:T(8,128)S(1)} %fusion.6, f32[2,1024,1024]{2,1,0:T(8,128)} %param.5), kind=kOutput, calls=%fused_computation.8 | convolution fusion | flops 12884901888 | bytes 12582912 | tf_op jit(solution)/shard_map/dot_general | solution.py:20
  579.5 5.5 copy.12
  585.0 4.7 select_multiply_fusion
  589.7 9.7 %fusion.77 = f32[1,128,1024]{1,2,0:T(8,128)S(1)} fusion(f32[128,1024]{0,1:T(8,128)} %reduce-scatter.2.cloned.1.call-done, f32[1,1024,1024]{2,1,0:T(8,128)} %all-gather.14.cloned.1.call-done, f32[1024,1024]{0,1:T(8,128)} %bitcast.95, s32[]{:T(128)S(6)} %select_n.105, f32[1024,1024]{0,1:T(8,128)} %select_multiply_fusion, f32[1,128,1024]{1,2,0:T(8,128)S(1)} %copy.22, ...), kind=kOutput, calls=%fused_computation.64 | convolution fusion | flops 1611530240 | bytes 7997952 | tf_op jit(solution)/shard_map/dot_general | solution.py:20
  599.4 0.1 pad_maximum_fusion
  599.5 1.3 copy.17
  (23 shorter events, 0.4 us)
Async XLA Ops:
  6.5 60.0 %all-reduce.13.cloned.1.call-start = ((), (), s32[]{:S(2)}) async-start(), calls=%async_computation.9 | async-start | bytes 2097152 | tf_op jit(solution)/shard_map/psum | solution.py:11
  11.5 139.1 %all-reduce.7.cloned.1.call-start = ((), (), s32[]{:S(2)}) async-start(), calls=%async_computation.2 | async-start | bytes 8388608 | tf_op jit(solution)/shard_map/psum | solution.py:29
  66.5 2.5 copy-start.2
  69.9 120.1 %all-gather.8.cloned.1.call-start = ((), (), s32[]{:S(2)}) async-start(), calls=%async_computation.1 | async-start | bytes 4718592 | tf_op jit(solution)/shard_map/all_gather | solution.py:59
  70.6 191.5 %all-gather.12.cloned.1.call-start = ((), (), s32[]{:S(2)}) async-start(), calls=%async_computation.6 | async-start | bytes 4718592 | tf_op jit(solution)/shard_map/all_gather | solution.py:58
  71.2 286.0 %all-reduce.11.cloned.1.call-start = ((), (), s32[]{:S(2)}) async-start(), calls=%async_computation.8 | async-start | bytes 4194304 | tf_op jit(solution)/shard_map/psum | solution.py:11
  269.5 125.4 %all-gather.14.cloned.1.call-start = ((), (), s32[]{:S(2)}) async-start(), calls=%async_computation.7 | async-start | bytes 4718592 | tf_op jit(solution)/shard_map/all_gather | solution.py:58
  271.4 208.0 %all-reduce.9.cloned.1.call-start = ((), (), s32[]{:S(2)}) async-start(), calls=%async_computation.3 | async-start | bytes 8388608 | tf_op jit(solution)/shard_map/psum | solution.py:29
  357.2 1.2 copy-start.1
  358.4 4.8 copy-start
  368.4 150.5 %all-gather.10.cloned.1.call-start = ((), (), s32[]{:S(2)}) async-start(), calls=%async_computation.5 | async-start | bytes 4718592 | tf_op jit(solution)/shard_map/all_gather | solution.py:59
  370.4 219.3 %reduce-scatter.2.cloned.1.call-start = ((), (), s32[]{:S(2)}) async-start(), calls=%async_computation.4 | async-start | bytes 4718592 | tf_op jit(solution)/shard_map/reduce_scatter | solution.py:68
Sparse Core Ops, SparseCore 0:
  11.6 54.8 all-reduce.12
  70.1 80.3 all-reduce.6
  152.4 37.4 all-gather.7
  191.7 37.4 all-gather.11
  269.6 87.5 all-reduce.10
  359.1 35.6 all-gather.13
  398.5 80.9 all-reduce.8
  481.4 37.4 all-gather.9
  522.3 51.3 reduce-scatter.1
where the time goes:
time: 614 us; the launch traced here: 608 us
  waiting for transfers between devices  393 us (64%)
  matrix products  150 us (24%)
  local copies, waits for them, and re-layouts  34.6 us (6%)
  other arithmetic  16.5 us (3%)
  between operations  13.6 us (2%)
    psum x2, waiting for transfers between devices, fixed_block(): diag_pre = jnp.tril(lax.psum(diag_term, 'col'))  153 us
    psum x2, waiting for transfers between devices, spread(): return lax.psum(kept, axis)  141 us
    dot_general x8, matrix products, product(): jnp.dot(left_mat, right_mat, precision=HIGHEST, preferred_element_type=jn...  126 us
    all_gather x2, waiting for transfers between devices, local(): diag_factor = lax.all_gather(held_fac[0], 'col', axis=0, tiled=True)  78.8 us
    dot_general x4, local copies, waits for them, and re-layouts, product(): jnp.dot(left_mat, right_mat, precision=HIGHEST, preferred_element_type=jn...  21.5 us
    all_gather x2, waiting for transfers between devices, local(): row_panel = lax.all_gather(factor_rows[panel], 'col', axis=0, tiled=True)  19.2 us
  transfers between devices with their start and end apart: 9, of which 7 were waited for; matrix products, arithmetic and copies ran while one was open for 29% of the time, Pallas kernels for 0%

commit v1 on v0

--- a/solution.py
+++ b/solution.py
@@ -1,9 +1,28 @@
+import functools
 import jax
 import jax.numpy as jnp
 from jax import lax
 from jax.sharding import PartitionSpec as P
 
 HIGHEST = lax.Precision.HIGHEST
+
+
+def _fill_cells(block_here, axis_id):
+    p_count = jax.lax.psum(1, axis_id)
+    fields = [block_here]
+    for t in range(p_count - 1):
+        back = jax.lax.ppermute(
+            fields[-1], axis_id, [(it, (it + 1) % p_count) for it in range(p_count)]
+        )
+        fields.append(back)
+    return jnp.roll(
+        jnp.concatenate(fields[::-1], axis=0),
+        (jax.lax.axis_index(axis_id) + 1) * block_here.shape[0],
+        axis=0,
+    )
+
+
+arrange_cubes = functools.partial(_fill_cells, axis_id="col")
 
 
 def spread(value, axis, source):
@@ -56,7 +75,7 @@
         )
         diag_term = placed - jnp.einsum("qbi,qbj->ij", col_adjoint, held_fac[1:], precision=HIGHEST)
         row_panel = lax.all_gather(factor_rows[panel], "col", axis=0, tiled=True)
-        diag_factor = lax.all_gather(held_fac[0], "col", axis=0, tiled=True)
+        diag_factor = arrange_cubes(held_fac[0])
         diag_new = fixed_block(diag_factor, diag_term, inverse)
         sym_rows = lax.dynamic_slice_in_dim(diag_new + diag_new.T, offset, slab_rows, 0)
         left_cols = (columns < first_col + panel * panel_width)[None, :]

time: 614 us -> 585 us (0.953)
  waiting for transfers between devices: 393 us -> 337 us
  local copies, waits for them, and re-layouts: 34.6 us -> 58.7 us
    ppermute x0 -> x14, waiting for transfers between devices: none -> 182 us  [_fill_cells(): jax.lax.ppermute(fields[-1], axis_id, [(it, (it + 1) % p_count) for it in...]
    psum x2, waiting for transfers between devices: 153 us -> 15.6 us  [fixed_block(): diag_pre = jnp.tril(lax.psum(diag_term, 'col'))]
    all_gather x2 -> x0, waiting for transfers between devices: 78.8 us -> none  [local(): diag_factor = lax.all_gather(held_fac[0], 'col', axis=0, tiled=True)]
    unnamed x9 -> x57, local copies, waits for them, and re-layouts: 2.64 us -> 25.6 us
    all_gather x2, waiting for transfers between devices: 19.2 us -> 0.02 us  [local(): row_panel = lax.all_gather(factor_rows[panel], 'col', axis=0, tiled=True)]
  transfers between devices with their start and end apart: 9 -> 21, of which waited for: 7 -> 17; matrix products, arithmetic and copies ran while one was open for 29% -> 34% of each run, Pallas kernels for 0% -> 0%
where the time goes in v1:
time: 585 us; the launch traced here: 577 us
  waiting for transfers between devices  337 us (58%)
  matrix products  149 us (25%)
  local copies, waits for them, and re-layouts  58.7 us (10%)
  other arithmetic  16.5 us (3%)
  between operations  14.3 us (2%)
    ppermute x14, waiting for transfers between devices, _fill_cells(): jax.lax.ppermute(fields[-1], axis_id, [(it, (it + 1) % p_count) for it in...  182 us
    psum x2, waiting for transfers between devices, spread(): return lax.psum(kept, axis)  139 us
    dot_general x8, matrix products, product(): jnp.dot(left_mat, right_mat, precision=HIGHEST, preferred_element_type=jn...  126 us
    unnamed x57, local copies, waits for them, and re-layouts  25.6 us
    dot_general x4, local copies, waits for them, and re-layouts, product(): jnp.dot(left_mat, right_mat, precision=HIGHEST, preferred_element_type=jn...  21.7 us
    psum x2, waiting for transfers between devices, fixed_block(): diag_pre = jnp.tril(lax.psum(diag_term, 'col'))  15.6 us
  transfers between devices with their start and end apart: 21, of which 17 were waited for; matrix products, arithmetic and copies ran while one was open for 34% of the time, Pallas kernels for 0%

profile of v1, /device:TPU:0, one launch (start us, length us, event | category | flops | bytes accessed | tf_op | source)
XLA Modules:
  0.0 577.3 jit_solution(16487623730557708800)
XLA Ops:
  6.5 1.5 copy.4
  8.1 1.3 fusion.119
  11.5 55.0 %all-reduce.13.cloned.1.call-done = (f32[128,1024]{0,1:T(8,128)}, f32[128,1024]{0,1:T(8,128)}) async-done(((f32[128,1024]{0,1:T(8,128)}, f32[128,1024]{0,1:T(8,128)}), (f32[128,1024]{0,1:T(8,128)}, f32[128,1024]{0,1:T(8,128)})) %all-reduce.13.cloned.1.call-update) | async-done | bytes 1048592 | tf_op jit(solution)/shard_map/psum | solution.py:30
  66.5 2.5 broadcast.54.clone
  70.7 12.0 %collective-permute-done.7 = f32[128,1024]{0,1:T(8,128)S(1)} collective-permute-done((f32[128,1024]{0,1:T(8,128)S(1)}, f32[128,1024]{0,1:T(8,128)S(1)}, u32[]{:S(2)}, u32[]{:S(2)}) %collective-permute-start.7) | collective-permute-done | bytes 524320 | tf_op jit(solution)/shard_map/ppermute | solution.py:14
  83.2 18.8 %collective-permute-done.8 = f32[128,1024]{0,1:T(8,128)S(1)} collective-permute-done((f32[128,1024]{0,1:T(8,128)S(1)}, f32[128,1024]{0,1:T(8,128)S(1)}, u32[]{:S(2)}, u32[]{:S(2)}) %collective-permute-start.8) | collective-permute-done | bytes 524320 | tf_op jit(solution)/shard_map/ppermute | solution.py:14
  102.8 14.0 %collective-permute-done.9 = f32[128,1024]{0,1:T(8,128)S(1)} collective-permute-done((f32[128,1024]{0,1:T(8,128)S(1)}, f32[128,1024]{0,1:T(8,128)S(1)}, u32[]{:S(2)}, u32[]{:S(2)}) %collective-permute-start.9) | collective-permute-done | bytes 524320 | tf_op jit(solution)/shard_map/ppermute | solution.py:14
  117.6 9.6 %collective-permute-done.10 = f32[128,1024]{0,1:T(8,128)S(1)} collective-permute-done((f32[128,1024]{0,1:T(8,128)S(1)}, f32[128,1024]{0,1:T(8,128)S(1)}, u32[]{:S(2)}, u32[]{:S(2)}) %collective-permute-start.10) | collective-permute-done | bytes 524320 | tf_op jit(solution)/shard_map/ppermute | solution.py:14
  128.0 10.7 %collective-permute-done.11 = f32[128,1024]{0,1:T(8,128)} collective-permute-done((f32[128,1024]{0,1:T(8,128)S(1)}, f32[128,1024]{0,1:T(8,128)}, u32[]{:S(2)}, u32[]{:S(2)}) %collective-permute-start.11) | collective-permute-done | bytes 524320 | tf_op jit(solution)/shard_map/ppermute | solution.py:14
  138.6 16.4 %collective-permute-done.12 = f32[128,1024]{0,1:T(8,128)} collective-permute-done((f32[128,1024]{0,1:T(8,128)}, f32[128,1024]{0,1:T(8,128)}, u32[]{:S(2)}, u32[]{:S(2)}) %collective-permute-start.12) | collective-permute-done | bytes 524320 | tf_op jit(solution)/shard_map/ppermute | solution.py:14
  155.3 1.3 iota_compare_fusion.1
  157.7 13.2 %collective-permute-done.13 = f32[128,1024]{0,1:T(8,128)} collective-permute-done((f32[128,1024]{0,1:T(8,128)}, f32[128,1024]{0,1:T(8,128)}, u32[]{:S(2)}, u32[]{:S(2)}) %collective-permute-start.13) | collective-permute-done | bytes 524320 | tf_op jit(solution)/shard_map/ppermute | solution.py:14
  170.9 1.9 constant_dynamic-update-slice_fusion.15
  172.8 1.9 constant_dynamic-update-slice_fusion.14
  174.7 1.9 constant_dynamic-update-slice_fusion.13
  181.1 17.8 %fusion.1 = f32[1024,1024]{1,0:T(8,128)} fusion(s32[]{:T(128)S(6)} %select_n.137, f32[1024,1024]{0,1:T(8,128)} %constant_dynamic-update-slice_fusion.8, f32[1024,1024]{0,1:T(8,128)} %all-reduce.7.cloned.1.call-done), kind=kOutput, calls=%fused_computation.5 | convolution fusion | flops 12888047616 | bytes 12582916 | tf_op jit(solution)/shard_map/dot_general | solution.py:39
  198.9 5.4 copy.8
  204.3 20.0 %fusion.23 = f32[1024,1024]{1,0:T(8,128)S(1)} fusion(f32[1024,1024]{1,0:T(8,128)} %fusion.1, f32[1024,1024]{0,1:T(8,128)} %copy.8, f32[2,1024,1024]{2,1,0:T(8,128)} %param.7), kind=kOutput, calls=%fused_computation.25 | convolution fusion | flops 12898533376 | bytes 16777216 | tf_op jit(solution)/shard_map/dot_general | solution.py:39
  224.2 16.8 %fusion.21 = f32[1024,1024]{1,0:T(8,128)} fusion(f32[1024,1024]{1,0:T(8,128)S(1)} %fusion.23, f32[2,1024,1024]{2,1,0:T(8,128)} %param.7), kind=kOutput, calls=%fused_computation.23 | convolution fusion | flops 12884901888 | bytes 12582912 | tf_op jit(solution)/shard_map/dot_general | solution.py:39
  241.1 5.3 copy.9
  246.4 6.5 %select_multiply_fusion.1 = (f32[1024,1024]{0,1:T(8,128)}, f32[1024,1024]{0,1:T(8,128)}) fusion(f32[1024,1024]{0,1:T(8,128)} %copy.9), kind=kLoop, calls=%fused_computation.34 | loop fusion | flops 9437184 | bytes 12582912 | tf_op jit(solution)/shard_map/mul | solution.py:35
  252.9 6.2 %fusion.53 = f32[128,1024]{0,1:T(8,128)S(1)} fusion(f32[1,1024,1024]{1,2,0:T(8,128)} %all-gather.5.cloned.1.call-done, f32[1024,1024]{0,1:T(8,128)} %bitcast.96, s32[]{:T(128)S(6)} %select_n.115, f32[1024,1024]{0,1:T(8,128)} %get-tuple-element.14, f32[1,128,1024]{1,2,0:T(8,128)S(1)} %copy.23, f32[1024,1024]{0,1:T(8,128)} %get-tuple-element.15, ...), kind=kOutput, calls=%fused_computation.60 | convolution fusion | flops 1611399168 | bytes 7473664 | tf_op jit(solution)/shard_map/dot_general | solution.py:39
  260.3 1.9 slice.43
  262.7 84.1 %all-reduce.11.cloned.1.call-done = (f32[2,128,1024]{1,2,0:T(8,128)}, f32[2,128,1024]{1,2,0:T(8,128)}) async-done(((f32[2,128,1024]{1,2,0:T(8,128)}, f32[2,128,1024]{1,2,0:T(8,128)}), (f32[2,128,1024]{1,2,0:T(8,128)}, f32[2,128,1024]{1,2,0:T(8,128)})) %all-reduce.11.cloned.1.call-update) | async-done | bytes 2097168 | tf_op jit(solution)/shard_map/psum | solution.py:30
  348.1 4.8 fusion.17
  352.8 5.1 convolution_subtract_fusion
  359.2 10.9 %collective-permute-done = f32[128,1024]{0,1:T(8,128)S(1)} collective-permute-done((f32[128,1024]{0,1:T(8,128)S(1)}, f32[128,1024]{0,1:T(8,128)S(1)}, u32[]{:S(2)}, u32[]{:S(2)}) %collective-permute-start) | collective-permute-done | bytes 524320 | tf_op jit(solution)/shard_map/ppermute | solution.py:14
  370.8 19.9 %collective-permute-done.1 = f32[128,1024]{0,1:T(8,128)S(1)} collective-permute-done((f32[128,1024]{0,1:T(8,128)S(1)}, f32[128,1024]{0,1:T(8,128)S(1)}, u32[]{:S(2)}, u32[]{:S(2)}) %collective-permute-start.1) | collective-permute-done | bytes 524320 | tf_op jit(solution)/shard_map/ppermute | solution.py:14
  390.7 5.0 fusion.92
  395.8 4.5 collective-permute-done.2
  400.3 20.6 %collective-permute-done.3 = f32[128,1024]{0,1:T(8,128)S(1)} collective-permute-done((f32[128,1024]{0,1:T(8,128)}, f32[128,1024]{0,1:T(8,128)S(1)}, u32[]{:S(2)}, u32[]{:S(2)}) %collective-permute-start.3) | collective-permute-done | bytes 524320 | tf_op jit(solution)/shard_map/ppermute | solution.py:14
  421.0 10.7 %collective-permute-done.4 = f32[128,1024]{0,1:T(8,128)S(1)} collective-permute-done((f32[128,1024]{0,1:T(8,128)S(1)}, f32[128,1024]{0,1:T(8,128)S(1)}, u32[]{:S(2)}, u32[]{:S(2)}) %collective-permute-start.4) | collective-permute-done | bytes 524320 | tf_op jit(solution)/shard_map/ppermute | solution.py:14
  431.6 15.2 %collective-permute-done.5 = f32[128,1024]{0,1:T(8,128)} collective-permute-done((f32[128,1024]{0,1:T(8,128)S(1)}, f32[128,1024]{0,1:T(8,128)}, u32[]{:S(2)}, u32[]{:S(2)}) %collective-permute-start.5) | collective-permute-done | bytes 524320 | tf_op jit(solution)/shard_map/ppermute | solution.py:14
  447.3 8.7 %fusion.68 = f32[1,128,1024]{1,2,0:T(8,128)S(1)} fusion(f32[128,1024]{0,1:T(8,128)S(1)} %copy.16, f32[128,1024]{0,1:T(8,128)S(1)} %fusion.53, f32[128,1024]{1,0:T(8,128)S(1)} %fusion.17, f32[1,1024,1024]{2,1,0:T(8,128)} %all-gather.7.cloned.1.call-done, pred[1024]{0:T(1024)(128)(4,1)S(1)} %fusion.100, pred[]{:T(512)S(6)} %eq.36), kind=kOutput, calls=%fused_computation.65 | convolution fusion | flops 1611005952 | bytes 6292481 | tf_op jit(solution)/shard_map/qib,bj->qij/dot_general | solution.py:95
  456.1 5.1 collective-permute-done.6
  461.2 1.9 constant_dynamic-update-slice_fusion.7
  463.1 1.9 constant_dynamic-update-slice_fusion.6
  465.0 1.9 constant_dynamic-update-slice_fusion.5
  467.9 2.1 constant_dynamic-update-slice_fusion.3
  472.5 15.6 %all-reduce.9.cloned.1.call-done = f32[1024,1024]{0,1:T(8,128)} async-done(((f32[1024,1024]{0,1:T(8,128)}), f32[1024,1024]{0,1:T(8,128)}) %all-reduce.9.cloned.1.call-update) | async-done | bytes 4194320 | tf_op jit(solution)/shard_map/psum | solution.py:48
  488.1 17.9 %fusion.4 = f32[1024,1024]{1,0:T(8,128)} fusion(s32[]{:T(128)S(6)} %select_n.137, f32[1024,1024]{0,1:T(8,128)} %constant_dynamic-update-slice_fusion, f32[1024,1024]{0,1:T(8,128)} %all-reduce.9.cloned.1.call-done), kind=kOutput, calls=%fused_computation.7 | convolution fusion | flops 12888047616 | bytes 12582916 | tf_op jit(solution)/shard_map/dot_general | solution.py:39
  506.0 5.4 copy.11
  511.3 20.4 %fusion.12 = f32[1024,1024]{1,0:T(8,128)S(1)} fusion(f32[1024,1024]{1,0:T(8,128)} %fusion.4, f32[1024,1024]{0,1:T(8,128)} %copy.11, f32[2,1024,1024]{2,1,0:T(8,128)} %param.7), kind=kOutput, calls=%fused_computation.15 | convolution fusion | flops 12898533376 | bytes 16777216 | tf_op jit(solution)/shard_map/dot_general | solution.py:39
  531.7 16.8 %fusion.14 = f32[1024,1024]{1,0:T(8,128)} fusion(f32[1024,1024]{1,0:T(8,128)S(1)} %fusion.12, f32[2,1024,1024]{2,1,0:T(8,128)} %param.7), kind=kOutput, calls=%fused_computation.16 | convolution fusion | flops 12884901888 | bytes 12582912 | tf_op jit(solution)/shard_map/dot_general | solution.py:39
  548.6 5.6 copy.12
  554.2 4.7 select_multiply_fusion
  558.9 9.7 %fusion.80 = f32[1,128,1024]{1,2,0:T(8,128)S(1)} fusion(f32[128,1024]{0,1:T(8,128)} %reduce-scatter.2.cloned.1.call-done, f32[1,1024,1024]{2,1,0:T(8,128)} %all-gather.7.cloned.1.call-done, f32[1024,1024]{0,1:T(8,128)} %bitcast.95, s32[]{:T(128)S(6)} %select_n.115, f32[1024,1024]{0,1:T(8,128)} %select_multiply_fusion, f32[1,128,1024]{1,2,0:T(8,128)S(1)} %copy.22, ...), kind=kOutput, calls=%fused_computation.69 | convolution fusion | flops 1611530240 | bytes 7997952 | tf_op jit(solution)/shard_map/dot_general | solution.py:39
  568.7 1.3 copy.17
  (95 shorter events, 21.3 us)
Async XLA Ops:
  6.5 60.0 %all-reduce.13.cloned.1.call-start = ((), (), s32[]{:S(2)}) async-start(), calls=%async_computation.7 | async-start | bytes 2097152 | tf_op jit(solution)/shard_map/psum | solution.py:30
  11.5 169.6 %all-reduce.7.cloned.1.call-start = ((), (), s32[]{:S(2)}) async-start(), calls=%async_computation.1 | async-start | bytes 8388608 | tf_op jit(solution)/shard_map/psum | solution.py:48
  66.5 2.5 copy-start.19
  66.5 3.4 copy-start.3
  69.9 183.0 %all-gather.5.cloned.1.call-start = ((), (), s32[]{:S(2)}) async-start(), calls=%async_computation.4 | async-start | bytes 4718592 | tf_op jit(solution)/shard_map/all_gather | solution.py:77
  70.0 12.8 %collective-permute-start.7 = (f32[128,1024]{0,1:T(8,128)S(1)}, f32[128,1024]{0,1:T(8,128)S(1)}, u32[]{:S(2)}, u32[]{:S(2)}) collective-permute-start(f32[128,1024]{0,1:T(8,128)S(1)} %copy-done.3), channel_id=1, source_target_pairs={{0,1},{1,2},{2,3},{3,4},{4,5},{5,6},{6,7},{7,0},{8,9},{9,10},{10,1... | collective-permute-start | bytes 1572872 | tf_op jit(solution)/shard_map/ppermute | solution.py:14
  70.6 276.1 %all-reduce.11.cloned.1.call-start = ((), (), s32[]{:S(2)}) async-start(), calls=%async_computation.6 | async-start | bytes 4194304 | tf_op jit(solution)/shard_map/psum | solution.py:30
  82.7 72.4 %copy-start.4 = (f32[128,1024]{0,1:T(8,128)}, f32[128,1024]{0,1:T(8,128)S(1)}, u32[]{:S(2)}) copy-start(f32[128,1024]{0,1:T(8,128)S(1)} %collective-permute-done.7) | copy-start | bytes 1572868
  82.7 19.3 %collective-permute-start.8 = (f32[128,1024]{0,1:T(8,128)S(1)}, f32[128,1024]{0,1:T(8,128)S(1)}, u32[]{:S(2)}, u32[]{:S(2)}) collective-permute-start(f32[128,1024]{0,1:T(8,128)S(1)} %collective-permute-done.7), channel_id=1, source_target_pairs={{0,1},{1,2},{2,3},{3,4},{4,5},{5,6},{6,7},{7,0},{8,9},{9,10},{10,1... | collective-permute-start | bytes 1572872 | tf_op jit(solution)/shard_map/ppermute | solution.py:14
  102.0 0.8 copy-start.6
  102.8 14.0 %collective-permute-start.9 = (f32[128,1024]{0,1:T(8,128)S(1)}, f32[128,1024]{0,1:T(8,128)S(1)}, u32[]{:S(2)}, u32[]{:S(2)}) collective-permute-start(f32[128,1024]{0,1:T(8,128)S(1)} %collective-permute-done.8), channel_id=1, source_target_pairs={{0,1},{1,2},{2,3},{3,4},{4,5},{5,6},{6,7},{7,0},{8,9},{9,10},{10,1... | collective-permute-start | bytes 1572872 | tf_op jit(solution)/shard_map/ppermute | solution.py:14
  116.8 0.8 copy-start.8
  117.6 9.6 %collective-permute-start.10 = (f32[128,1024]{0,1:T(8,128)S(1)}, f32[128,1024]{0,1:T(8,128)S(1)}, u32[]{:S(2)}, u32[]{:S(2)}) collective-permute-start(f32[128,1024]{0,1:T(8,128)S(1)} %collective-permute-done.9), channel_id=1, source_target_pairs={{0,1},{1,2},{2,3},{3,4},{4,5},{5,6},{6,7},{7,0},{8,9},{9,10},{10,1... | collective-permute-start | bytes 1572872 | tf_op jit(solution)/shard_map/ppermute | solution.py:14
  127.2 0.8 copy-start.12
  128.0 10.7 %collective-permute-start.11 = (f32[128,1024]{0,1:T(8,128)S(1)}, f32[128,1024]{0,1:T(8,128)}, u32[]{:S(2)}, u32[]{:S(2)}) collective-permute-start(f32[128,1024]{0,1:T(8,128)S(1)} %collective-permute-done.10), channel_id=1, source_target_pairs={{0,1},{1,2},{2,3},{3,4},{4,5},{5,6},{6,7},{7,0},{8,9},{9,10},{10,1... | collective-permute-start | bytes 1572872 | tf_op jit(solution)/shard_map/ppermute | solution.py:14
  138.6 16.4 %collective-permute-start.12 = (f32[128,1024]{0,1:T(8,128)}, f32[128,1024]{0,1:T(8,128)}, u32[]{:S(2)}, u32[]{:S(2)}) collective-permute-start(f32[128,1024]{0,1:T(8,128)} %collective-permute-done.11), channel_id=1, source_target_pairs={{0,1},{1,2},{2,3},{3,4},{4,5},{5,6},{6,7},{7,0},{8,9},{9,10},{10,1... | collective-permute-start | bytes 1572872 | tf_op jit(solution)/shard_map/ppermute | solution.py:14
  155.1 15.9 %collective-permute-start.13 = (f32[128,1024]{0,1:T(8,128)}, f32[128,1024]{0,1:T(8,128)}, u32[]{:S(2)}, u32[]{:S(2)}) collective-permute-start(f32[128,1024]{0,1:T(8,128)} %collective-permute-done.12), channel_id=1, source_target_pairs={{0,1},{1,2},{2,3},{3,4},{4,5},{5,6},{6,7},{7,0},{8,9},{9,10},{10,1... | collective-permute-start | bytes 1572872 | tf_op jit(solution)/shard_map/ppermute | solution.py:14
  155.3 21.3 %copy-start.13 = (f32[128,1024]{0,1:T(8,128)S(1)}, f32[128,1024]{0,1:T(8,128)}, u32[]{:S(2)}) copy-start(f32[128,1024]{0,1:T(8,128)} %copy-done.12) | copy-start | bytes 1572868
  155.3 22.2 %copy-start.9 = (f32[128,1024]{0,1:T(8,128)S(1)}, f32[128,1024]{0,1:T(8,128)}, u32[]{:S(2)}) copy-start(f32[128,1024]{0,1:T(8,128)} %copy-done.8) | copy-start | bytes 1572868
  155.3 23.1 %copy-start.7 = (f32[128,1024]{0,1:T(8,128)S(1)}, f32[128,1024]{0,1:T(8,128)}, u32[]{:S(2)}) copy-start(f32[128,1024]{0,1:T(8,128)} %copy-done.6) | copy-start | bytes 1572868
  156.6 22.7 %copy-start.5 = (f32[128,1024]{0,1:T(8,128)S(1)}, f32[128,1024]{0,1:T(8,128)}, u32[]{:S(2)}) copy-start(f32[128,1024]{0,1:T(8,128)} %copy-done.4) | copy-start | bytes 1572868
  260.2 187.0 %all-gather.7.cloned.1.call-start = ((), (), s32[]{:S(2)}) async-start(), calls=%async_computation.5 | async-start | bytes 4718592 | tf_op jit(solution)/shard_map/all_gather | solution.py:77
  262.2 225.9 %all-reduce.9.cloned.1.call-start = ((), (), s32[]{:S(2)}) async-start(), calls=%async_computation.2 | async-start | bytes 8388608 | tf_op jit(solution)/shard_map/psum | solution.py:48
  346.8 1.2 copy-start.2
  348.0 4.8 copy-start
  358.0 200.9 %reduce-scatter.2.cloned.1.call-start = ((), (), s32[]{:S(2)}) async-start(), calls=%async_computation.3 | async-start | bytes 4718592 | tf_op jit(solution)/shard_map/reduce_scatter | solution.py:87
  359.1 10.9 %collective-permute-start = (f32[128,1024]{0,1:T(8,128)S(1)}, f32[128,1024]{0,1:T(8,128)S(1)}, u32[]{:S(2)}, u32[]{:S(2)}) collective-permute-start(f32[128,1024]{0,1:T(8,128)S(1)} %slice_bitcast_fusion.5), channel_id=1, source_target_pairs={{0,1},{1,2},{2,3},{3,4},{4,5},{5,6},{6,7},{7,0},{8,9},{9,10},{10,1... | collective-permute-start | bytes 1572872 | tf_op jit(solution)/shard_map/ppermute | solution.py:14
  370.0 0.8 copy-start.10
  370.8 19.9 %collective-permute-start.1 = (f32[128,1024]{0,1:T(8,128)S(1)}, f32[128,1024]{0,1:T(8,128)S(1)}, u32[]{:S(2)}, u32[]{:S(2)}) collective-permute-start(f32[128,1024]{0,1:T(8,128)S(1)} %collective-permute-done), channel_id=1, source_target_pairs={{0,1},{1,2},{2,3},{3,4},{4,5},{5,6},{6,7},{7,0},{8,9},{9,10},{10,1... | collective-permute-start | bytes 1572872 | tf_op jit(solution)/shard_map/ppermute | solution.py:14
  390.7 5.1 copy-start.14
  390.7 9.6 %collective-permute-start.2 = (f32[128,1024]{0,1:T(8,128)S(1)}, f32[128,1024]{0,1:T(8,128)}, u32[]{:S(2)}, u32[]{:S(2)}) collective-permute-start(f32[128,1024]{0,1:T(8,128)S(1)} %collective-permute-done.1), channel_id=1, source_target_pairs={{0,1},{1,2},{2,3},{3,4},{4,5},{5,6},{6,7},{7,0},{8,9},{9,10},{10,1... | collective-permute-start | bytes 1572872 | tf_op jit(solution)/shard_map/ppermute | solution.py:14
  400.3 20.6 %collective-permute-start.3 = (f32[128,1024]{0,1:T(8,128)}, f32[128,1024]{0,1:T(8,128)S(1)}, u32[]{:S(2)}, u32[]{:S(2)}) collective-permute-start(f32[128,1024]{0,1:T(8,128)} %collective-permute-done.2), channel_id=1, source_target_pairs={{0,1},{1,2},{2,3},{3,4},{4,5},{5,6},{6,7},{7,0},{8,9},{9,10},{10,1... | collective-permute-start | bytes 1572872 | tf_op jit(solution)/shard_map/ppermute | solution.py:14
  421.0 26.1 %copy-start.16 = (f32[128,1024]{0,1:T(8,128)}, f32[128,1024]{0,1:T(8,128)S(1)}, u32[]{:S(2)}) copy-start(f32[128,1024]{0,1:T(8,128)S(1)} %collective-permute-done.3) | copy-start | bytes 1572868
  421.0 10.7 %collective-permute-start.4 = (f32[128,1024]{0,1:T(8,128)S(1)}, f32[128,1024]{0,1:T(8,128)S(1)}, u32[]{:S(2)}, u32[]{:S(2)}) collective-permute-start(f32[128,1024]{0,1:T(8,128)S(1)} %collective-permute-done.3), channel_id=1, source_target_pairs={{0,1},{1,2},{2,3},{3,4},{4,5},{5,6},{6,7},{7,0},{8,9},{9,10},{10,1... | collective-permute-start | bytes 1572872 | tf_op jit(solution)/shard_map/ppermute | solution.py:14
  431.6 15.7 %copy-start.18 = (f32[128,1024]{0,1:T(8,128)}, f32[128,1024]{0,1:T(8,128)S(1)}, u32[]{:S(2)}) copy-start(f32[128,1024]{0,1:T(8,128)S(1)} %collective-permute-done.4) | copy-start | bytes 1572868
  431.6 15.2 %collective-permute-start.5 = (f32[128,1024]{0,1:T(8,128)S(1)}, f32[128,1024]{0,1:T(8,128)}, u32[]{:S(2)}, u32[]{:S(2)}) collective-permute-start(f32[128,1024]{0,1:T(8,128)S(1)} %collective-permute-done.4), channel_id=1, source_target_pairs={{0,1},{1,2},{2,3},{3,4},{4,5},{5,6},{6,7},{7,0},{8,9},{9,10},{10,1... | collective-permute-start | bytes 1572872 | tf_op jit(solution)/shard_map/ppermute | solution.py:14
  446.8 14.4 %collective-permute-start.6 = (f32[128,1024]{0,1:T(8,128)}, f32[128,1024]{0,1:T(8,128)}, u32[]{:S(2)}, u32[]{:S(2)}) collective-permute-start(f32[128,1024]{0,1:T(8,128)} %collective-permute-done.5), channel_id=1, source_target_pairs={{0,1},{1,2},{2,3},{3,4},{4,5},{5,6},{6,7},{7,0},{8,9},{9,10},{10,1... | collective-permute-start | bytes 1572872 | tf_op jit(solution)/shard_map/ppermute | solution.py:14
  447.3 19.7 %copy-start.17 = (f32[128,1024]{0,1:T(8,128)S(1)}, f32[128,1024]{0,1:T(8,128)}, u32[]{:S(2)}) copy-start(f32[128,1024]{0,1:T(8,128)} %copy-done.16) | copy-start | bytes 1572868
  456.0 13.9 %copy-start.15 = (f32[128,1024]{0,1:T(8,128)S(1)}, f32[128,1024]{0,1:T(8,128)}, u32[]{:S(2)}) copy-start(f32[128,1024]{0,1:T(8,128)} %copy-done.14) | copy-start | bytes 1572868
  456.0 14.7 %copy-start.11 = (f32[128,1024]{0,1:T(8,128)S(1)}, f32[128,1024]{0,1:T(8,128)}, u32[]{:S(2)}) copy-start(f32[128,1024]{0,1:T(8,128)} %copy-done.10) | copy-start | bytes 1572868
  456.0 15.6 %copy-start.1 = (f32[2,128,1024]{1,2,0:T(8,128)S(1)}, f32[2,128,1024]{1,2,0:T(8,128)}, u32[]{:S(2)}) copy-start(f32[2,128,1024]{1,2,0:T(8,128)} %get-tuple-element.7) | copy-start | bytes 3145732
Sparse Core Ops, SparseCore 0:
  11.6 54.8 all-reduce.12
  70.1 98.5 all-reduce.6
  170.6 36.5 all-gather.4
  260.3 86.3 all-reduce.10
  348.7 42.5 all-gather.6
  394.7 93.3 all-reduce.8
  491.5 51.3 reduce-scatter.1
